TPU v7x, 256 devices: a whole 4x4x8 slice. The times are simulated.
256 devices in a mesh: req: 8 (over z), exp: 8 (over y, core), hid: 4 (over x).
Axes of the slice: x: 4, y: 4, z: 8, core: 2. Of those that a mesh axis runs over, the one named last changes fastest.
Arguments:
- layer_input_rows: bfloat16 [16384, 1536], P(('req', 'exp')), may hold values from -6 to 6
- attention_norm_gain: float32 [1536], replicated
- query_weight: bfloat16 [1536, 1536], P(None, 'hid'), may hold values from -1 to 1
- key_weight: bfloat16 [1536, 512], P(None, 'hid'), may hold values from -1 to 1
- value_weight: bfloat16 [1536, 512], P(None, 'hid'), may hold values from -0.15625 to 0.15625
- attention_output_weight: bfloat16 [1536, 1536], P('hid'), may hold values from -0.15625 to 0.15625
- query_down_factor: bfloat16 [64, 1536, 16], P(('req', 'exp')), may hold values from -0.15625 to 0.15625
- query_up_factor: bfloat16 [64, 16, 1536], P(('req', 'exp')), may hold values from -1.5 to 1.5
- value_down_factor: bfloat16 [64, 1536, 16], P(('req', 'exp')), may hold values from -0.15625 to 0.15625
- value_up_factor: bfloat16 [64, 16, 512], P(('req', 'exp')), may hold values from -1.5 to 1.5
- lengths: int32 [8, 4], P('req'), may hold values from 1 to 1024, 2048 in all within a row
- request_adapter: int32 [8, 4], replicated, may hold values from 0 to 63
- adapter_home_row: int32 [64], replicated, may hold values from 0 to 63, each once
- expert_norm_gain: float32 [1536], replicated, may hold values from 0.4 to 1.6
- routes: int32 [16384, 8], P(('req', 'exp', 'hid')), may hold values from 0 to 39, all different within a row; in each aligned block of 64 rows (0 to 63, 64 to 127, ...) at most 16 rows name the same one
- router_expert_weight: float32 [16384, 8], P(('req', 'exp', 'hid')), may hold values from 0.1 to 0.5
- expert_gate_weight: bfloat16 [40, 1536, 512], P('exp', None, 'hid'), may hold values from -0.15625 to 0.15625
- expert_up_weight: bfloat16 [40, 1536, 512], P('exp', None, 'hid'), may hold values from -0.15625 to 0.15625
- expert_down_weight: bfloat16 [40, 512, 1536], P('exp', 'hid'), may hold values from -0.25 to 0.25
Outputs:
- attn_out: bfloat16 [16384, 1536], P(('req', 'exp', 'hid'))
- expert_out: bfloat16 [16384, 1536], P(('req', 'exp', 'hid'))
Inputs may be any that keep to these rules, and one draw needn't show every extreme that they name: `lengths`: each row sums to 2048; its largest entry is exactly 1024. `adapter_home_row`: each adapter row appears once. `routes`: A row names 8 different experts. In the rows of one device (64 consecutive rows, aligned) no expert is named more than 16 times, a bound that some block reaches in some of them.
All inputs are finite; a program needn't handle non-finite values.
Results may differ from a plain program's by a relative error of at most 0.029.
The roundings to bfloat16 on the way count: a program that leaves them out, or rounds other values in their place, can miss the bound.
Values may be sent and summed in bfloat16 or wider, within the bound.
No kernel may reach another device: no remote copies, remote signals or barrier semaphores. Data moves between devices by JAX's collectives and lax.ppermute only.
A program may use at most 128 MiB of HBM per device.

v0:
```python
import jax
import jax.numpy as jnp
from jax import lax
from jax.sharding import PartitionSpec as P

HEAD_WIDTH = 64
scale_attn = 0.015625
residual_mult = 0.22
norm_eps = 1e-06
rope_base = 10000.0
neg_large = -1e30


def rms_norm(values, norm_gain):
    widened = values.astype(jnp.float32)
    mean_sq = jnp.mean(widened * widened, axis=-1, keepdims=True)
    return (widened * lax.rsqrt(mean_sq + norm_eps) * norm_gain).astype(jnp.bfloat16)


def rotary(heads_in, position):
    half_size = heads_in.shape[-1] // 2
    frequency = rope_base ** (-2.0 * jnp.arange(half_size, dtype=jnp.float32) / heads_in.shape[-1])
    angles = position.astype(jnp.float32)[:, None] * frequency[None, :]
    cosine = jnp.cos(angles)[:, None, :]
    sine_part = jnp.sin(angles)[:, None, :]
    first_half = heads_in[..., :half_size]
    second_half = heads_in[..., half_size:]
    return jnp.concatenate(
        [
            first_half * cosine - second_half * sine_part,
            second_half * cosine + first_half * sine_part,
        ],
        axis=-1,
    )


def request_of(row_ids, group_len):
    request_end = jnp.cumsum(group_len)
    return jnp.sum((row_ids[:, None] >= request_end[None, :]).astype(jnp.int32), axis=1)


def locate(row_ids, group_len):
    request_end = jnp.cumsum(group_len)
    request_start = request_end - group_len
    request = request_of(row_ids, group_len)
    member = request[:, None] == jnp.arange(group_len.shape[0], dtype=jnp.int32)[None, :]
    position = row_ids - jnp.sum(jnp.where(member, request_start[None, :], 0), axis=1)
    return (request, member, position)


def expert_rows(rows_in, expert_gate_weight, expert_up_weight, expert_down_weight):
    gate_act = jnp.einsum(
        "red,edf->ref", rows_in, expert_gate_weight, preferred_element_type=jnp.float32
    )
    upper = jnp.einsum(
        "red,edf->ref", rows_in, expert_up_weight, preferred_element_type=jnp.float32
    )
    hidden = (jax.nn.silu(gate_act) * upper).astype(jnp.bfloat16)
    return jnp.einsum(
        "ref,efd->red", hidden, expert_down_weight, preferred_element_type=jnp.float32
    )


def per_device(
    layer_input_rows,
    attention_norm_gain,
    query_weight,
    key_weight,
    value_weight,
    attention_output_weight,
    query_down_factor,
    query_up_factor,
    value_down_factor,
    value_up_factor,
    lengths,
    request_adapter,
    adapter_home_row,
    expert_norm_gain,
    routes,
    router_expert_weight,
    expert_gate_weight,
    expert_up_weight,
    expert_down_weight,
):
    exp_count = lax.axis_size("exp")
    hid_count = lax.axis_size("hid")
    exp_index = lax.axis_index("exp")
    hid_index = lax.axis_index("hid")
    req_index = lax.axis_index("req")
    query_rows = layer_input_rows.shape[0]
    width = layer_input_rows.shape[1]
    kv_local = key_weight.shape[1] // HEAD_WIDTH
    q_local = query_weight.shape[1] // HEAD_WIDTH
    group_share = q_local // kv_local
    adapter_rank_size = query_down_factor.shape[2]
    requests = lengths.shape[1]
    group_len = lengths[0]
    row_ids = exp_index * query_rows + jnp.arange(query_rows, dtype=jnp.int32)
    request, member, position = locate(row_ids, group_len)
    wanted = lax.dynamic_index_in_dim(request_adapter, req_index, 0, keepdims=False)
    slot_ids = jnp.arange(adapter_home_row.shape[0], dtype=jnp.int32)
    home_of = jnp.sum(
        jnp.where(wanted[:, None] == slot_ids[None, :], adapter_home_row[None, :], 0), axis=1
    )
    query_cols = q_local * HEAD_WIDTH
    kv_cols = kv_local * HEAD_WIDTH
    bank_local = query_down_factor.shape[0]
    up_q = lax.dynamic_slice_in_dim(query_up_factor, hid_index * query_cols, query_cols, 2)
    up_v = lax.dynamic_slice_in_dim(value_up_factor, hid_index * kv_cols, kv_cols, 2)
    parts_in = (query_down_factor, up_q, value_down_factor, up_v)
    part_shapes = [p.shape[1:] for p in parts_in]
    part_sizes = [p.shape[1] * p.shape[2] for p in parts_in]
    bank = jnp.concatenate([p.reshape(bank_local, -1) for p in parts_in], axis=1)
    along_req = lax.all_gather(bank, "req", axis=0, tiled=True)
    home_dev = home_of // bank_local
    home_pick = home_dev // exp_count * bank_local + home_of % bank_local
    mine = home_dev % exp_count == exp_index
    rows_pick = jnp.take(along_req, home_pick, axis=0)
    rows_pick = jnp.where(mine[:, None], rows_pick, jnp.zeros_like(rows_pick))
    rows_all = lax.all_to_all(
        jnp.broadcast_to(rows_pick[None], (exp_count,) + rows_pick.shape),
        "exp",
        split_axis=0,
        concat_axis=0,
        tiled=True,
    )
    rows_pick = rows_all[home_dev % exp_count, jnp.arange(requests, dtype=jnp.int32)]
    chosen = []
    start = 0
    for shape_in, size_in in zip(part_shapes, part_sizes):
        chosen.append(rows_pick[:, start : start + size_in].reshape((requests,) + shape_in))
        start += size_in
    qa_sel, qb_sel, va_sel, vb_sel = chosen
    normed_rows = rms_norm(layer_input_rows, attention_norm_gain)

    def low_rank_term(a_sel, b_sel, width_cols, offset):
        inner_terms = jnp.einsum(
            "td,jdr->tjr", normed_rows, a_sel, preferred_element_type=jnp.float32
        )
        inner_terms = (
            jnp.where(member[:, :, None], inner_terms, 0.0)
            .reshape(query_rows, requests * adapter_rank_size)
            .astype(jnp.bfloat16)
        )
        right_factor = b_sel.reshape(requests * adapter_rank_size, width_cols)
        return jnp.dot(inner_terms, right_factor, preferred_element_type=jnp.float32)

    query_matrix = jnp.dot(
        normed_rows, query_weight, preferred_element_type=jnp.float32
    ) + low_rank_term(qa_sel, qb_sel, query_cols, hid_index * query_cols)
    query_matrix = rotary(query_matrix.reshape(query_rows, q_local, HEAD_WIDTH), position).astype(
        jnp.bfloat16
    )
    query_matrix = query_matrix.reshape(query_rows, kv_local, group_share, HEAD_WIDTH)
    keys_own = jnp.dot(normed_rows, key_weight, preferred_element_type=jnp.float32)
    keys_own = (
        rotary(keys_own.reshape(query_rows, kv_local, HEAD_WIDTH), position)
        .astype(jnp.bfloat16)
        .reshape(query_rows, kv_cols)
    )
    values_own = jnp.dot(
        normed_rows, value_weight, preferred_element_type=jnp.float32
    ) + low_rank_term(va_sel, vb_sel, kv_cols, hid_index * kv_cols)
    values_own = values_own.astype(jnp.bfloat16)
    running_max = jnp.full((kv_local, group_share, query_rows), neg_large, jnp.float32)
    kv_own = jnp.concatenate([keys_own, values_own], axis=1)
    kv_piece = lax.all_to_all(
        jnp.broadcast_to(kv_own[None], (exp_count,) + kv_own.shape),
        "exp",
        split_axis=0,
        concat_axis=0,
        tiled=True,
    ).reshape(exp_count * query_rows, 2 * kv_cols)
    key_piece = kv_piece[:, :kv_cols]
    value_piece = kv_piece[:, kv_cols:]
    piece_len = key_piece.shape[0]
    key_ids = jnp.arange(piece_len, dtype=jnp.int32)
    key_request = request_of(key_ids, group_len)
    allowed = (request[:, None] == key_request[None, :]) & (key_ids[None, :] <= row_ids[:, None])
    key_heads = key_piece.reshape(piece_len, kv_local, HEAD_WIDTH)
    value_heads = value_piece.reshape(piece_len, kv_local, HEAD_WIDTH)
    scores = (
        jnp.einsum("qkgh,nkh->kgqn", query_matrix, key_heads, preferred_element_type=jnp.float32)
        * scale_attn
    )
    scores = jnp.where(allowed[None, None], scores, neg_large)
    new_max = jnp.maximum(running_max, jnp.max(scores, axis=-1))
    weights = jnp.where(allowed[None, None], jnp.exp(scores - new_max[..., None]), 0.0)
    running_sum = jnp.sum(weights, axis=-1)
    running_out = jnp.einsum(
        "kgqn,nkh->kgqh",
        weights.astype(jnp.bfloat16),
        value_heads,
        preferred_element_type=jnp.float32,
    )
    running_max, running_sum, running_out = (new_max, running_sum, running_out)
    attended = (running_out / running_sum[..., None]).astype(jnp.bfloat16)
    attended = jnp.transpose(attended, (2, 0, 1, 3)).reshape(query_rows, query_cols)
    tok_rows = query_rows // hid_count
    head_sums = jnp.dot(attended, attention_output_weight, preferred_element_type=jnp.float32)
    head_sums = head_sums.astype(jnp.bfloat16).reshape(hid_count, tok_rows, width)
    head_sums = lax.all_to_all(head_sums, "hid", split_axis=0, concat_axis=0, tiled=True)
    attn_out = jnp.sum(head_sums.astype(jnp.float32), axis=0).astype(jnp.bfloat16)
    own_rows = lax.dynamic_slice_in_dim(layer_input_rows, hid_index * tok_rows, tok_rows, 0)
    mixed_rows = own_rows.astype(jnp.float32) + residual_mult * attn_out.astype(jnp.float32)
    normed_moe = rms_norm(mixed_rows, expert_norm_gain)
    local_exp = expert_gate_weight.shape[0]
    expert_count = local_exp * exp_count
    top_count = routes.shape[1]
    capacity = max(2, tok_rows // 4)
    flat_route = routes.reshape(tok_rows * top_count)
    route_hits = (flat_route[:, None] == jnp.arange(expert_count, dtype=jnp.int32)[None, :]).astype(
        jnp.int32
    )
    earlier = jnp.cumsum(route_hits, axis=0) - route_hits
    slot_pos = jnp.sum(earlier * route_hits, axis=1)
    slots = slot_pos * expert_count + flat_route
    slot_table = jnp.arange(capacity * expert_count, dtype=jnp.int32)
    placed = jnp.any(
        slot_table[:, None, None] == slots.reshape(tok_rows, top_count)[None], axis=2
    ).astype(jnp.bfloat16)
    outgoing = jnp.dot(placed, normed_moe, preferred_element_type=jnp.float32).astype(jnp.bfloat16)
    outgoing = outgoing.reshape(capacity, expert_count, width)
    partners = exp_count * hid_count
    halves = 2 if capacity % 2 == 0 else 1
    cap_part = capacity // halves
    slot_hit = slots.reshape(tok_rows, top_count)[:, :, None] == slot_table[None, None, :]
    combine = jnp.sum(jnp.where(slot_hit, router_expert_weight[:, :, None], 0.0), axis=1)
    expert_acc = jnp.zeros((tok_rows, width), jnp.float32)
    for half in range(halves):
        part_out = outgoing[half * cap_part : (half + 1) * cap_part]
        copies = jnp.broadcast_to(
            part_out.reshape(cap_part, exp_count, 1, local_exp, width),
            (cap_part, exp_count, hid_count, local_exp, width),
        )
        copies = copies.reshape(cap_part, partners * local_exp, width)
        arrived = lax.all_to_all(copies, ("exp", "hid"), split_axis=1, concat_axis=0, tiled=True)
        partials = expert_rows(
            arrived, expert_gate_weight, expert_up_weight, expert_down_weight
        ).astype(jnp.bfloat16)
        partials = jnp.transpose(
            partials.reshape(partners, cap_part, local_exp, width), (1, 0, 2, 3)
        ).reshape(cap_part, partners * local_exp, width)
        returned = lax.all_to_all(partials, ("exp", "hid"), split_axis=1, concat_axis=1, tiled=True)
        returned = returned.reshape(cap_part, exp_count, hid_count, local_exp, width)
        results = jnp.sum(returned.astype(jnp.float32), axis=2).astype(jnp.bfloat16)
        results = results.reshape(cap_part * expert_count, width)
        part_cols = combine[
            :, half * cap_part * expert_count : (half + 1) * cap_part * expert_count
        ]
        expert_acc = expert_acc + jnp.dot(
            part_cols,
            results.astype(jnp.float32),
            precision=lax.Precision.HIGHEST,
            preferred_element_type=jnp.float32,
        )
    expert_out = expert_acc.astype(jnp.bfloat16)
    return (attn_out, expert_out)


def solution(mesh):
    in_specs = (
        P(("req", "exp"), None),
        P(),
        P(None, "hid"),
        P(None, "hid"),
        P(None, "hid"),
        P("hid", None),
        P(("req", "exp"), None, None),
        P(("req", "exp"), None, None),
        P(("req", "exp"), None, None),
        P(("req", "exp"), None, None),
        P("req", None),
        P(),
        P(),
        P(),
        P(("req", "exp", "hid"), None),
        P(("req", "exp", "hid"), None),
        P("exp", None, "hid"),
        P("exp", None, "hid"),
        P("exp", "hid", None),
    )
    out_specs = (P(("req", "exp", "hid"), None), P(("req", "exp", "hid"), None))
    return jax.shard_map(
        per_device, mesh=mesh, in_specs=in_specs, out_specs=out_specs, check_vma=False
    )
```

profile of v0, /device:TPU:3, one launch (start us, length us, event | category | flops | bytes accessed | tf_op | source)
XLA Modules:
  0.0 396.5 jit_solution(12851483804816842418)
XLA Ops:
  5.1 28.5 %all-gather = bf16[8,1,57344]{2,1,0:T(2,128)(2,1)S(1)} all-gather(bf16[1,1,57344]{2,1,0:T(2,128)(2,1)S(1)} %maximum_bitcast_fusion), channel_id=1, replica_groups=mesh['req'=8,'exp'=8,'hid'=4] {'req'}, dimensions={0}, use_global_device_ids=true | all-gather | bytes 1032192 | tf_op jit(solution)/shard_map/all_gather | solution.py:114
  39.2 9.0 %all-to-all-start = ((bf16[8,4,57344]{2,1,0:T(4,128)(2,1)}), bf16[8,4,57344]{2,1,0:T(4,128)(2,1)}, u32[]{:S(2)}, u32[]{:S(2)}) async-start(bf16[8,4,57344]{2,1,0:T(4,128)(2,1)} %broadcast_in_dim.172), calls=%async_computation | async-start | bytes 7340032 | tf_op jit(solution)/shard_map/all_to_all | solution.py:120
  53.8 37.6 %all-to-all-done = bf16[8,4,57344]{2,1,0:T(4,128)(2,1)} async-done(((bf16[8,4,57344]{2,1,0:T(4,128)(2,1)}), bf16[8,4,57344]{2,1,0:T(4,128)(2,1)}, u32[]{:S(2)}, u32[]{:S(2)}) %all-to-all-start) | async-done | bytes 3670048 | tf_op jit(solution)/shard_map/all_to_all | solution.py:120
  109.3 4.4 %all-to-all-start.1 = ((bf16[8,256,256]{1,2,0:T(8,128)(2,1)}), bf16[8,256,256]{1,2,0:T(8,128)(2,1)S(1)}, u32[]{:S(2)}, u32[]{:S(2)}) async-start(bf16[8,256,256]{1,2,0:T(8,128)(2,1)} %broadcast_in_dim.174), calls=%async_computation.1 | async-start | bytes 2097152 | tf_op jit(solution)/shard_map/all_to_all | solution.py:167
  122.8 5.9 %all-to-all-done.1 = bf16[8,256,256]{1,2,0:T(8,128)(2,1)S(1)} async-done(((bf16[8,256,256]{1,2,0:T(8,128)(2,1)}), bf16[8,256,256]{1,2,0:T(8,128)(2,1)S(1)}, u32[]{:S(2)}, u32[]{:S(2)}) %all-to-all-start.1) | async-done | bytes 1048608 | tf_op jit(solution)/shard_map/all_to_all | solution.py:167
  138.7 3.6 fusion.57
  143.8 4.4 %all-to-all-start.2 = ((bf16[4,64,1536]{2,1,0:T(8,128)(2,1)}), bf16[4,64,1536]{2,1,0:T(8,128)(2,1)S(1)}, u32[]{:S(2)}, u32[]{:S(2)}) async-start(bf16[4,64,1536]{2,1,0:T(8,128)(2,1)} %bitcast.32), calls=%async_computation.2 | async-start | bytes 1572864 | tf_op jit(solution)/shard_map/all_to_all | solution.py:202
  150.6 7.5 %all-to-all-done.2 = bf16[4,64,1536]{2,1,0:T(8,128)(2,1)S(1)} async-done(((bf16[4,64,1536]{2,1,0:T(8,128)(2,1)}), bf16[4,64,1536]{2,1,0:T(8,128)(2,1)S(1)}, u32[]{:S(2)}, u32[]{:S(2)}) %all-to-all-start.2) | async-done | bytes 786464 | tf_op jit(solution)/shard_map/all_to_all | solution.py:202
  166.9 7.6 %all-to-all-start.3 = ((bf16[8,160,1536]{2,0,1:T(8,128)(2,1)}), bf16[8,160,1536]{2,0,1:T(8,128)(2,1)}, u32[]{:S(2)}, u32[]{:S(2)}) async-start(bf16[8,160,1536]{2,0,1:T(8,128)(2,1)} %bitcast.213), calls=%async_computation.3 | async-start | bytes 7864320 | tf_op jit(solution)/shard_map/all_to_all | solution.py:237
  177.7 44.9 %all-to-all-done.3 = bf16[8,160,1536]{2,0,1:T(8,128)(2,1)} async-done(((bf16[8,160,1536]{2,0,1:T(8,128)(2,1)}), bf16[8,160,1536]{2,0,1:T(8,128)(2,1)}, u32[]{:S(2)}, u32[]{:S(2)}) %all-to-all-start.3) | async-done | bytes 3932192 | tf_op jit(solution)/shard_map/all_to_all | solution.py:237
  226.1 5.1 %all-to-all-start.5 = ((bf16[8,160,1536]{2,0,1:T(8,128)(2,1)}), bf16[8,160,1536]{2,0,1:T(8,128)(2,1)}, u32[]{:S(2)}, u32[]{:S(2)}) async-start(bf16[8,160,1536]{2,0,1:T(8,128)(2,1)} %bitcast.212), calls=%async_computation.5 | async-start | bytes 7864320 | tf_op jit(solution)/shard_map/all_to_all | solution.py:237
  231.2 3.9 fusion.26
  235.1 6.8 %fusion.14 = bf16[32,8,5,1536]{3,1,0,2:T(8,128)(2,1)} fusion(bf16[5,128,1536]{2,1,0:T(8,128)(2,1)S(1)} %copy-done, bf16[5,1536,128]{2,1,0:T(8,128)(2,1)} %param.36, bf16[32,8,5,1536]{3,1,2,0:T(8,128)(2,1)} %bitcast.36, f32[256,5,128]{2,0,1:T(8,128)S(1)} %fusion.26), kind=kOutput, calls=%fused_computation.19 | convolution fusion | flops 1009582080 | bytes 12451840 | tf_op jit(solution)/shard_map/ref,efd->red/dot_general | solution.py:59
  241.9 4.3 %copy.103 = bf16[32,8,5,1536]{3,1,2,0:T(8,128)(2,1)} copy(bf16[32,8,5,1536]{3,1,0,2:T(8,128)(2,1)} %fusion.14) | data formatting | bytes 7864320 | tf_op jit(solution)/shard_map/reshape | solution.py:242
  246.3 32.8 %all-to-all-done.5 = bf16[8,160,1536]{2,0,1:T(8,128)(2,1)} async-done(((bf16[8,160,1536]{2,0,1:T(8,128)(2,1)}), bf16[8,160,1536]{2,0,1:T(8,128)(2,1)}, u32[]{:S(2)}, u32[]{:S(2)}) %all-to-all-start.5) | async-done | bytes 3932192 | tf_op jit(solution)/shard_map/all_to_all | solution.py:237
  279.1 5.1 %all-to-all-start.4 = ((bf16[8,160,1536]{2,0,1:T(8,128)(2,1)}), bf16[8,160,1536]{2,0,1:T(8,128)(2,1)}, u32[]{:S(2)}, u32[]{:S(2)}) async-start(bf16[8,160,1536]{2,0,1:T(8,128)(2,1)} %bitcast.211), calls=%async_computation.4 | async-start | bytes 7864320 | tf_op jit(solution)/shard_map/all_to_all | solution.py:244
  284.2 3.9 fusion.32
  288.1 6.9 %fusion.15 = bf16[32,8,5,1536]{3,1,0,2:T(8,128)(2,1)} fusion(bf16[5,128,1536]{2,1,0:T(8,128)(2,1)S(1)} %copy-done, bf16[5,1536,128]{2,1,0:T(8,128)(2,1)} %param.36, bf16[32,8,5,1536]{3,1,2,0:T(8,128)(2,1)} %bitcast.47, f32[256,5,128]{2,0,1:T(8,128)S(1)} %fusion.32), kind=kOutput, calls=%fused_computation.20 | convolution fusion | flops 1009582080 | bytes 12451840 | tf_op jit(solution)/shard_map/ref,efd->red/dot_general | solution.py:59
  295.0 4.3 %copy.107 = bf16[32,8,5,1536]{3,1,2,0:T(8,128)(2,1)} copy(bf16[32,8,5,1536]{3,1,0,2:T(8,128)(2,1)} %fusion.15) | data formatting | bytes 7864320 | tf_op jit(solution)/shard_map/reshape | solution.py:242
  299.3 32.9 %all-to-all-done.4 = bf16[8,160,1536]{2,0,1:T(8,128)(2,1)} async-done(((bf16[8,160,1536]{2,0,1:T(8,128)(2,1)}), bf16[8,160,1536]{2,0,1:T(8,128)(2,1)}, u32[]{:S(2)}, u32[]{:S(2)}) %all-to-all-start.4) | async-done | bytes 3932192 | tf_op jit(solution)/shard_map/all_to_all | solution.py:244
  332.2 5.2 %all-to-all-start.6 = ((bf16[8,160,1536]{2,0,1:T(8,128)(2,1)}), bf16[8,160,1536]{2,0,1:T(8,128)(2,1)}, u32[]{:S(2)}, u32[]{:S(2)}) async-start(bf16[8,160,1536]{2,0,1:T(8,128)(2,1)} %bitcast.210), calls=%async_computation.6 | async-start | bytes 7864320 | tf_op jit(solution)/shard_map/all_to_all | solution.py:244
  338.7 4.0 %reduce_sum.130 = bf16[8,8,5,1536]{3,0,2,1:T(8,128)(2,1)} reduce(bf16[8,8,4,5,1536]{4,0,3,2,1:T(8,128)(2,1)} %bitcast.44, bf16[]{:T(256)} %constant.140.clone.1), dimensions={2}, to_apply=%region_15.16 | reduce | flops 1474560 | bytes 4915202 | tf_op jit(solution)/shard_map/reduce_sum | solution.py:246
  345.4 40.0 %all-to-all-done.6 = bf16[8,160,1536]{2,0,1:T(8,128)(2,1)} async-done(((bf16[8,160,1536]{2,0,1:T(8,128)(2,1)}), bf16[8,160,1536]{2,0,1:T(8,128)(2,1)}, u32[]{:S(2)}, u32[]{:S(2)}) %all-to-all-start.6) | async-done | bytes 3932192 | tf_op jit(solution)/shard_map/all_to_all | solution.py:244
  385.4 4.0 %reduce_sum.131 = bf16[8,8,5,1536]{3,0,2,1:T(8,128)(2,1)} reduce(bf16[8,8,4,5,1536]{4,0,3,2,1:T(8,128)(2,1)} %bitcast.55, bf16[]{:T(256)} %constant.140.clone.1), dimensions={2}, to_apply=%region_16.17 | reduce | flops 1474560 | bytes 4915202 | tf_op jit(solution)/shard_map/reduce_sum | solution.py:246
  (164 shorter events, 82.4 us)
Async XLA Ops:
  0.6 234.5 %copy-start = (bf16[5,128,1536]{2,1,0:T(8,128)(2,1)S(1)}, bf16[5,128,1536]{2,1,0:T(8,128)(2,1)}, u32[]{:S(2)}) copy-start(bf16[5,128,1536]{2,1,0:T(8,128)(2,1)} %param.37) | copy-start | bytes 5898244
  5.1 29.6 %copy-start.24 = (s32[8,4]{0,1:T(4,128)S(1)}, s32[8,4]{0,1:T(4,128)}, u32[]{:S(2)}) copy-start(s32[8,4]{0,1:T(4,128)} %param.30) | copy-start | bytes 388
  5.1 29.8 %copy-start.32 = (s32[64]{0:T(128)S(1)}, s32[64]{0:T(128)}, u32[]{:S(2)}) copy-start(s32[64]{0:T(128)} %param.31) | copy-start | bytes 772
  39.2 9.0 %copy-start.33 = (s32[1,4]{1,0:T(1,128)S(1)}, s32[1,4]{1,0:T(1,128)}, u32[]{:S(2)}) copy-start(s32[1,4]{1,0:T(1,128)} %param.29) | copy-start | bytes 52
  39.2 9.2 %copy-start.22 = (s32[64,8]{0,1:T(8,128)S(1)}, s32[64,8]{0,1:T(8,128)}, u32[]{:S(2)}) copy-start(s32[64,8]{0,1:T(8,128)} %param.33) | copy-start | bytes 6148
  39.2 10.9 %copy-start.4 = (bf16[256,1536]{1,0:T(8,128)(2,1)S(1)}, bf16[256,1536]{1,0:T(8,128)(2,1)}, u32[]{:S(2)}) copy-start(bf16[256,1536]{1,0:T(8,128)(2,1)} %param.19) | copy-start | bytes 2359300
  39.2 11.4 %copy-start.28 = (bf16[1536,128]{1,0:T(8,128)(2,1)S(1)}, bf16[1536,128]{1,0:T(8,128)(2,1)}, u32[]{:S(2)}) copy-start(bf16[1536,128]{1,0:T(8,128)(2,1)} %param.22) | copy-start | bytes 1179652
  39.2 11.4 %copy-start.30 = (f32[1536]{0:T(1024)S(1)}, f32[1536]{0:T(1024)}, u32[]{:S(2)}) copy-start(f32[1536]{0:T(1024)} %param.20) | copy-start | bytes 18436
  39.2 52.2 %all-to-all-start = ((bf16[8,4,57344]{2,1,0:T(4,128)(2,1)}), bf16[8,4,57344]{2,1,0:T(4,128)(2,1)}, u32[]{:S(2)}, u32[]{:S(2)}) async-start(bf16[8,4,57344]{2,1,0:T(4,128)(2,1)} %broadcast_in_dim.172), calls=%async_computation | async-start | bytes 7340032 | tf_op jit(solution)/shard_map/all_to_all | solution.py:120
  48.5 5.3 %copy-start.7 = (s32[64,8]{1,0:T(8,128)}, s32[64,8]{1,0:T(8,128)S(1)}, u32[]{:S(2)}) copy-start(s32[64,8]{1,0:T(8,128)S(1)} %copy.96) | copy-start | bytes 6148
  50.3 48.3 %copy-start.25 = (f32[256]{0:T(256)}, f32[256]{0:T(256)S(1)}, u32[]{:S(2)}) copy-start(f32[256]{0:T(256)S(1)} %add_rsqrt_fusion) | copy-start | bytes 3076
  108.2 5.5 %copy-start.15 = (s32[2048]{0:T(1024)S(1)}, s32[2048]{0:T(1024)}, u32[]{:S(2)}) copy-start(s32[2048]{0:T(1024)} %convert_reduce_fusion) | copy-start | bytes 24580
  108.2 5.5 %copy-start.17 = (s32[256]{0:T(256)S(1)}, s32[256]{0:T(256)}, u32[]{:S(2)}) copy-start(s32[256]{0:T(256)} %copy-done.16) | copy-start | bytes 3076
  108.2 5.5 %copy-start.21 = (s32[256]{0:T(256)S(1)}, s32[256]{0:T(256)}, u32[]{:S(2)}) copy-start(s32[256]{0:T(256)} %copy-done.20) | copy-start | bytes 3076
  109.3 19.4 %all-to-all-start.1 = ((bf16[8,256,256]{1,2,0:T(8,128)(2,1)}), bf16[8,256,256]{1,2,0:T(8,128)(2,1)S(1)}, u32[]{:S(2)}, u32[]{:S(2)}) async-start(bf16[8,256,256]{1,2,0:T(8,128)(2,1)} %broadcast_in_dim.174), calls=%async_computation.1 | async-start | bytes 2097152 | tf_op jit(solution)/shard_map/all_to_all | solution.py:167
  142.3 5.9 %copy-start.19 = (s32[4,128]{1,0:T(4,128)S(1)}, s32[4,128]{1,0:T(4,128)}, u32[]{:S(2)}) copy-start(s32[4,128]{1,0:T(4,128)} %eq.130) | copy-start | bytes 6148
  142.3 5.9 %copy-start.8 = (s32[64,8]{1,0:T(8,128)S(1)}, s32[64,8]{1,0:T(8,128)}, u32[]{:S(2)}) copy-start(s32[64,8]{1,0:T(8,128)} %copy-done.7) | copy-start | bytes 6148
  143.8 15.7 %copy-start.18 = (f32[1536]{0:T(1024)S(1)}, f32[1536]{0:T(1024)}, u32[]{:S(2)}) copy-start(f32[1536]{0:T(1024)} %param.32) | copy-start | bytes 18436
  143.8 14.4 %all-to-all-start.2 = ((bf16[4,64,1536]{2,1,0:T(8,128)(2,1)}), bf16[4,64,1536]{2,1,0:T(8,128)(2,1)S(1)}, u32[]{:S(2)}, u32[]{:S(2)}) async-start(bf16[4,64,1536]{2,1,0:T(8,128)(2,1)} %bitcast.32), calls=%async_computation.2 | async-start | bytes 1572864 | tf_op jit(solution)/shard_map/all_to_all | solution.py:202
  166.9 55.7 %all-to-all-start.3 = ((bf16[8,160,1536]{2,0,1:T(8,128)(2,1)}), bf16[8,160,1536]{2,0,1:T(8,128)(2,1)}, u32[]{:S(2)}, u32[]{:S(2)}) async-start(bf16[8,160,1536]{2,0,1:T(8,128)(2,1)} %bitcast.213), calls=%async_computation.3 | async-start | bytes 7864320 | tf_op jit(solution)/shard_map/all_to_all | solution.py:237
  226.1 53.0 %all-to-all-start.5 = ((bf16[8,160,1536]{2,0,1:T(8,128)(2,1)}), bf16[8,160,1536]{2,0,1:T(8,128)(2,1)}, u32[]{:S(2)}, u32[]{:S(2)}) async-start(bf16[8,160,1536]{2,0,1:T(8,128)(2,1)} %bitcast.212), calls=%async_computation.5 | async-start | bytes 7864320 | tf_op jit(solution)/shard_map/all_to_all | solution.py:237
  279.1 53.1 %all-to-all-start.4 = ((bf16[8,160,1536]{2,0,1:T(8,128)(2,1)}), bf16[8,160,1536]{2,0,1:T(8,128)(2,1)}, u32[]{:S(2)}, u32[]{:S(2)}) async-start(bf16[8,160,1536]{2,0,1:T(8,128)(2,1)} %bitcast.211), calls=%async_computation.4 | async-start | bytes 7864320 | tf_op jit(solution)/shard_map/all_to_all | solution.py:244
  332.2 5.4 %copy-start.11 = (s32[64,8]{1,0:T(8,128)S(1)}, s32[64,8]{1,0:T(8,128)}, u32[]{:S(2)}) copy-start(s32[64,8]{1,0:T(8,128)} %copy-done.10) | copy-start | bytes 6148
  332.2 53.2 %all-to-all-start.6 = ((bf16[8,160,1536]{2,0,1:T(8,128)(2,1)}), bf16[8,160,1536]{2,0,1:T(8,128)(2,1)}, u32[]{:S(2)}, u32[]{:S(2)}) async-start(bf16[8,160,1536]{2,0,1:T(8,128)(2,1)} %bitcast.210), calls=%async_computation.6 | async-start | bytes 7864320 | tf_op jit(solution)/shard_map/all_to_all | solution.py:244
  (18 other events, 51.6 us)
where the time goes:
time: 398 us; the launch traced here: 397 us
  waiting for transfers between devices  202 us (51%)
  local copies, waits for them, and re-layouts  57.4 us (14%)
  matrix products  44.1 us (11%)
  starting transfers between devices  40.9 us (10%)
  blocking collectives  28.5 us (7%)
  other arithmetic  22.6 us (6%)
    all_to_all x2, waiting for transfers between devices, per_device(): lax.all_to_all(copies, ('exp', 'hid'), split_axis=1, concat_axis=0, tiled...  77.8 us
    all_to_all x2, waiting for transfers between devices, per_device(): lax.all_to_all(partials, ('exp', 'hid'), split_axis=1, concat_axis=1, til...  72.8 us
    all_to_all x1, waiting for transfers between devices, per_device(): lax.all_to_all(jnp.broadcast_to(rows_pick[None], (exp_count,) + rows_pick...  37.6 us
    all_gather x1, blocking collectives, per_device(): along_req = lax.all_gather(bank, 'req', axis=0, tiled=True)  28.5 us
    dot_general x2, matrix products, expert_rows(): jnp.einsum('ref,efd->red', hidden, expert_down_weight, preferred_element_...  13.7 us
    all_to_all x2, starting transfers between devices, per_device(): lax.all_to_all(copies, ('exp', 'hid'), split_axis=1, concat_axis=0, tiled...  12.7 us
    broadcast_in_dim x6, local copies, waits for them, and re-layouts, per_device(): jnp.broadcast_to(part_out.reshape(cap_part, exp_count, 1, local_exp, widt...  10.9 us
    all_to_all x2, starting transfers between devices, per_device(): lax.all_to_all(partials, ('exp', 'hid'), split_axis=1, concat_axis=1, til...  10.4 us
  transfers between devices with their start and end apart: 7, of which 7 were waited for; matrix products, arithmetic and copies ran while one was open for 15% of the time, Pallas kernels for 0%

commit v1 on v0

--- a/solution.py
+++ b/solution.py
@@ -111,7 +111,9 @@
     part_shapes = [p.shape[1:] for p in parts_in]
     part_sizes = [p.shape[1] * p.shape[2] for p in parts_in]
     bank = jnp.concatenate([p.reshape(bank_local, -1) for p in parts_in], axis=1)
-    along_req = lax.all_gather(bank, "req", axis=0, tiled=True)
+    along_req = jnp.concatenate(
+        lax.all_to_all(jnp.stack([bank] * lax.axis_size("req")), "req", 0, 0), axis=0
+    )
     home_dev = home_of // bank_local
     home_pick = home_dev // exp_count * bank_local + home_of % bank_local
     mine = home_dev % exp_count == exp_index

time: 398 us -> 425 us (1.068); the launches traced: 397 us -> 417 us
  blocking collectives: 28.5 us -> 0 us
  waiting for transfers between devices: 202 us -> 227 us
  local copies, waits for them, and re-layouts: 57.4 us -> 66.6 us
  other arithmetic: 22.6 us -> 30.6 us
  starting transfers between devices: 40.9 us -> 46.7 us
    all_gather x1 -> x0, blocking collectives: 28.5 us -> none  [per_device(): along_req = lax.all_gather(bank, 'req', axis=0, tiled=True)]
    all_to_all x0 -> x1, waiting for transfers between devices: none -> 25.9 us  [per_device(): lax.all_to_all(jnp.stack([bank] * lax.axis_size('req')), 'req', 0, 0)]
    all_to_all x0 -> x1, starting transfers between devices: none -> 8.74 us  [per_device(): lax.all_to_all(jnp.stack([bank] * lax.axis_size('req')), 'req', 0, 0)]
    another operation x5 -> x6, other arithmetic: 3.16 us -> 10.7 us  [the longest x1 7.52 us: per_device(): jnp.stack([bank] * lax.axis_size('req'))]
    unnamed x77 -> x79, local copies, waits for them, and re-layouts: 5.17 us -> 11.6 us
  transfers between devices with their start and end apart: 7 -> 8, of which waited for: 7 -> 8; matrix products, arithmetic and copies ran while one was open for 15% -> 14% of each run, Pallas kernels for 0% -> 0%
where the time goes in v1:
time: 425 us; the launch traced here: 417 us
  waiting for transfers between devices  227 us (53%)
  local copies, waits for them, and re-layouts  66.6 us (16%)
  starting transfers between devices  46.7 us (11%)
  matrix products  44.1 us (10%)
  other arithmetic  30.6 us (7%)
    all_to_all x2, waiting for transfers between devices, per_device(): lax.all_to_all(copies, ('exp', 'hid'), split_axis=1, concat_axis=0, tiled...  77.6 us
    all_to_all x2, waiting for transfers between devices, per_device(): lax.all_to_all(partials, ('exp', 'hid'), split_axis=1, concat_axis=1, til...  72.6 us
    all_to_all x1, waiting for transfers between devices, per_device(): lax.all_to_all(jnp.broadcast_to(rows_pick[None], (exp_count,) + rows_pick...  37.6 us
    all_to_all x1, waiting for transfers between devices, per_device(): lax.all_to_all(jnp.stack([bank] * lax.axis_size('req')), 'req', 0, 0)  25.9 us
    dot_general x2, matrix products, expert_rows(): jnp.einsum('ref,efd->red', hidden, expert_down_weight, preferred_element_...  13.7 us
    all_to_all x2, starting transfers between devices, per_device(): lax.all_to_all(copies, ('exp', 'hid'), split_axis=1, concat_axis=0, tiled...  13 us
    unnamed x79, local copies, waits for them, and re-layouts  11.6 us
    broadcast_in_dim x6, local copies, waits for them, and re-layouts, per_device(): jnp.broadcast_to(part_out.reshape(cap_part, exp_count, 1, local_exp, widt...  10.9 us
  transfers between devices with their start and end apart: 8, of which 8 were waited for; matrix products, arithmetic and copies ran while one was open for 14% of the time, Pallas kernels for 0%

profile of v1, /device:TPU:3, one launch (start us, length us, event | category | flops | bytes accessed | tf_op | source)
XLA Modules:
  0.0 416.7 jit_solution(8997145442299503796)
XLA Ops:
  8.2 7.5 %reduce.9 = bf16[8,57344]{1,0:T(8,128)(2,1)S(1)} reduce(bf16[8,1,57344]{2,1,0:T(2,128)(2,1)} %stack.2, bf16[]{:T(256)} %broadcast.484), dimensions={1}, to_apply=%stack.2.reduce_sub_computation | reduce | bytes 1835010 | tf_op jit(solution)/shard_map/stack | solution.py:115
  17.5 8.7 %all-to-all-start = ((bf16[8,2,28672]{2,1,0:T(2,128)(2,1)}), bf16[8,2,28672]{2,1,0:T(2,128)(2,1)S(1)}, u32[]{:S(2)}, u32[]{:S(2)}) async-start(bf16[8,2,28672]{2,1,0:T(2,128)(2,1)} %reshape.472), calls=%async_computation | async-start | bytes 1835008 | tf_op jit(solution)/shard_map/all_to_all | solution.py:115
  26.6 25.9 %all-to-all-done = bf16[8,2,28672]{2,1,0:T(2,128)(2,1)S(1)} async-done(((bf16[8,2,28672]{2,1,0:T(2,128)(2,1)}), bf16[8,2,28672]{2,1,0:T(2,128)(2,1)S(1)}, u32[]{:S(2)}, u32[]{:S(2)}) %all-to-all-start) | async-done | bytes 917536 | tf_op jit(solution)/shard_map/all_to_all | solution.py:115
  62.5 5.1 %all-to-all-start.1 = ((bf16[8,4,57344]{2,1,0:T(4,128)(2,1)}), bf16[8,4,57344]{2,1,0:T(4,128)(2,1)}, u32[]{:S(2)}, u32[]{:S(2)}) async-start(bf16[8,4,57344]{2,1,0:T(4,128)(2,1)} %broadcast_in_dim.172), calls=%async_computation.1 | async-start | bytes 7340032 | tf_op jit(solution)/shard_map/all_to_all | solution.py:122
  73.1 37.6 %all-to-all-done.1 = bf16[8,4,57344]{2,1,0:T(4,128)(2,1)} async-done(((bf16[8,4,57344]{2,1,0:T(4,128)(2,1)}), bf16[8,4,57344]{2,1,0:T(4,128)(2,1)}, u32[]{:S(2)}, u32[]{:S(2)}) %all-to-all-start.1) | async-done | bytes 3670048 | tf_op jit(solution)/shard_map/all_to_all | solution.py:122
  128.6 4.6 %all-to-all-start.2 = ((bf16[8,256,256]{1,2,0:T(8,128)(2,1)}), bf16[8,256,256]{1,2,0:T(8,128)(2,1)S(1)}, u32[]{:S(2)}, u32[]{:S(2)}) async-start(bf16[8,256,256]{1,2,0:T(8,128)(2,1)} %broadcast_in_dim.174), calls=%async_computation.2 | async-start | bytes 2097152 | tf_op jit(solution)/shard_map/all_to_all | solution.py:169
  142.4 5.8 %all-to-all-done.2 = bf16[8,256,256]{1,2,0:T(8,128)(2,1)S(1)} async-done(((bf16[8,256,256]{1,2,0:T(8,128)(2,1)}), bf16[8,256,256]{1,2,0:T(8,128)(2,1)S(1)}, u32[]{:S(2)}, u32[]{:S(2)}) %all-to-all-start.2) | async-done | bytes 1048608 | tf_op jit(solution)/shard_map/all_to_all | solution.py:169
  163.3 4.4 %all-to-all-start.3 = ((bf16[4,64,1536]{2,1,0:T(8,128)(2,1)}), bf16[4,64,1536]{2,1,0:T(8,128)(2,1)S(1)}, u32[]{:S(2)}, u32[]{:S(2)}) async-start(bf16[4,64,1536]{2,1,0:T(8,128)(2,1)} %bitcast.31), calls=%async_computation.3 | async-start | bytes 1572864 | tf_op jit(solution)/shard_map/all_to_all | solution.py:204
  170.1 7.5 %all-to-all-done.3 = bf16[4,64,1536]{2,1,0:T(8,128)(2,1)S(1)} async-done(((bf16[4,64,1536]{2,1,0:T(8,128)(2,1)}), bf16[4,64,1536]{2,1,0:T(8,128)(2,1)S(1)}, u32[]{:S(2)}, u32[]{:S(2)}) %all-to-all-start.3) | async-done | bytes 786464 | tf_op jit(solution)/shard_map/all_to_all | solution.py:204
  186.4 7.6 %all-to-all-start.4 = ((bf16[8,160,1536]{2,0,1:T(8,128)(2,1)}), bf16[8,160,1536]{2,0,1:T(8,128)(2,1)}, u32[]{:S(2)}, u32[]{:S(2)}) async-start(bf16[8,160,1536]{2,0,1:T(8,128)(2,1)} %bitcast.211), calls=%async_computation.4 | async-start | bytes 7864320 | tf_op jit(solution)/shard_map/all_to_all | solution.py:239
  197.2 44.9 %all-to-all-done.4 = bf16[8,160,1536]{2,0,1:T(8,128)(2,1)} async-done(((bf16[8,160,1536]{2,0,1:T(8,128)(2,1)}), bf16[8,160,1536]{2,0,1:T(8,128)(2,1)}, u32[]{:S(2)}, u32[]{:S(2)}) %all-to-all-start.4) | async-done | bytes 3932192 | tf_op jit(solution)/shard_map/all_to_all | solution.py:239
  245.6 5.4 %all-to-all-start.6 = ((bf16[8,160,1536]{2,0,1:T(8,128)(2,1)}), bf16[8,160,1536]{2,0,1:T(8,128)(2,1)}, u32[]{:S(2)}, u32[]{:S(2)}) async-start(bf16[8,160,1536]{2,0,1:T(8,128)(2,1)} %bitcast.210), calls=%async_computation.6 | async-start | bytes 7864320 | tf_op jit(solution)/shard_map/all_to_all | solution.py:239
  251.1 3.9 fusion.26
  255.0 6.8 %fusion.14 = bf16[32,8,5,1536]{3,1,0,2:T(8,128)(2,1)} fusion(bf16[5,128,1536]{2,1,0:T(8,128)(2,1)S(1)} %copy-done, bf16[5,1536,128]{2,1,0:T(8,128)(2,1)} %param.36, bf16[32,8,5,1536]{3,1,2,0:T(8,128)(2,1)} %bitcast.35, f32[256,5,128]{2,0,1:T(8,128)S(1)} %fusion.26), kind=kOutput, calls=%fused_computation.19 | convolution fusion | flops 1009582080 | bytes 12451840 | tf_op jit(solution)/shard_map/ref,efd->red/dot_general | solution.py:59
  261.8 4.3 %copy.103 = bf16[32,8,5,1536]{3,1,2,0:T(8,128)(2,1)} copy(bf16[32,8,5,1536]{3,1,0,2:T(8,128)(2,1)} %fusion.14) | data formatting | bytes 7864320 | tf_op jit(solution)/shard_map/reshape | solution.py:244
  266.2 32.6 %all-to-all-done.6 = bf16[8,160,1536]{2,0,1:T(8,128)(2,1)} async-done(((bf16[8,160,1536]{2,0,1:T(8,128)(2,1)}), bf16[8,160,1536]{2,0,1:T(8,128)(2,1)}, u32[]{:S(2)}, u32[]{:S(2)}) %all-to-all-start.6) | async-done | bytes 3932192 | tf_op jit(solution)/shard_map/all_to_all | solution.py:239
  298.8 5.1 %all-to-all-start.5 = ((bf16[8,160,1536]{2,0,1:T(8,128)(2,1)}), bf16[8,160,1536]{2,0,1:T(8,128)(2,1)}, u32[]{:S(2)}, u32[]{:S(2)}) async-start(bf16[8,160,1536]{2,0,1:T(8,128)(2,1)} %bitcast.209), calls=%async_computation.5 | async-start | bytes 7864320 | tf_op jit(solution)/shard_map/all_to_all | solution.py:246
  307.8 6.9 %fusion.15 = bf16[32,8,5,1536]{3,1,0,2:T(8,128)(2,1)} fusion(bf16[5,128,1536]{2,1,0:T(8,128)(2,1)S(1)} %copy-done, bf16[5,1536,128]{2,1,0:T(8,128)(2,1)} %param.36, bf16[32,8,5,1536]{3,1,2,0:T(8,128)(2,1)} %bitcast.46, f32[256,5,128]{2,0,1:T(8,128)S(1)} %fusion.32), kind=kOutput, calls=%fused_computation.20 | convolution fusion | flops 1009582080 | bytes 12451840 | tf_op jit(solution)/shard_map/ref,efd->red/dot_general | solution.py:59
  314.7 4.3 %copy.107 = bf16[32,8,5,1536]{3,1,2,0:T(8,128)(2,1)} copy(bf16[32,8,5,1536]{3,1,0,2:T(8,128)(2,1)} %fusion.15) | data formatting | bytes 7864320 | tf_op jit(solution)/shard_map/reshape | solution.py:244
  319.0 32.9 %all-to-all-done.5 = bf16[8,160,1536]{2,0,1:T(8,128)(2,1)} async-done(((bf16[8,160,1536]{2,0,1:T(8,128)(2,1)}), bf16[8,160,1536]{2,0,1:T(8,128)(2,1)}, u32[]{:S(2)}, u32[]{:S(2)}) %all-to-all-start.5) | async-done | bytes 3932192 | tf_op jit(solution)/shard_map/all_to_all | solution.py:246
  351.9 5.7 %all-to-all-start.7 = ((bf16[8,160,1536]{2,0,1:T(8,128)(2,1)}), bf16[8,160,1536]{2,0,1:T(8,128)(2,1)}, u32[]{:S(2)}, u32[]{:S(2)}) async-start(bf16[8,160,1536]{2,0,1:T(8,128)(2,1)} %bitcast.208), calls=%async_computation.7 | async-start | bytes 7864320 | tf_op jit(solution)/shard_map/all_to_all | solution.py:246
  358.8 4.0 reduce_sum.130
  365.6 39.7 %all-to-all-done.7 = bf16[8,160,1536]{2,0,1:T(8,128)(2,1)} async-done(((bf16[8,160,1536]{2,0,1:T(8,128)(2,1)}), bf16[8,160,1536]{2,0,1:T(8,128)(2,1)}, u32[]{:S(2)}, u32[]{:S(2)}) %all-to-all-start.7) | async-done | bytes 3932192 | tf_op jit(solution)/shard_map/all_to_all | solution.py:246
  405.3 4.0 reduce_sum.131
  (170 shorter events, 99.6 us)
Async XLA Ops:
  0.6 254.3 %copy-start = (bf16[5,128,1536]{2,1,0:T(8,128)(2,1)S(1)}, bf16[5,128,1536]{2,1,0:T(8,128)(2,1)}, u32[]{:S(2)}) copy-start(bf16[5,128,1536]{2,1,0:T(8,128)(2,1)} %param.37) | copy-start | bytes 5898244
  15.8 10.5 %copy-start.24 = (s32[8,4]{0,1:T(4,128)S(1)}, s32[8,4]{0,1:T(4,128)}, u32[]{:S(2)}) copy-start(s32[8,4]{0,1:T(4,128)} %param.30) | copy-start | bytes 388
  15.8 10.6 %copy-start.32 = (s32[64]{0:T(128)S(1)}, s32[64]{0:T(128)}, u32[]{:S(2)}) copy-start(s32[64]{0:T(128)} %param.31) | copy-start | bytes 772
  17.5 35.1 %all-to-all-start = ((bf16[8,2,28672]{2,1,0:T(2,128)(2,1)}), bf16[8,2,28672]{2,1,0:T(2,128)(2,1)S(1)}, u32[]{:S(2)}, u32[]{:S(2)}) async-start(bf16[8,2,28672]{2,1,0:T(2,128)(2,1)} %reshape.472), calls=%async_computation | async-start | bytes 1835008 | tf_op jit(solution)/shard_map/all_to_all | solution.py:115
  62.4 5.3 %copy-start.22 = (s32[64,8]{0,1:T(8,128)S(1)}, s32[64,8]{0,1:T(8,128)}, u32[]{:S(2)}) copy-start(s32[64,8]{0,1:T(8,128)} %param.33) | copy-start | bytes 6148
  62.4 7.0 %copy-start.4 = (bf16[256,1536]{1,0:T(8,128)(2,1)S(1)}, bf16[256,1536]{1,0:T(8,128)(2,1)}, u32[]{:S(2)}) copy-start(bf16[256,1536]{1,0:T(8,128)(2,1)} %param.19) | copy-start | bytes 2359300
  62.4 7.4 %copy-start.28 = (bf16[1536,128]{1,0:T(8,128)(2,1)S(1)}, bf16[1536,128]{1,0:T(8,128)(2,1)}, u32[]{:S(2)}) copy-start(bf16[1536,128]{1,0:T(8,128)(2,1)} %param.22) | copy-start | bytes 1179652
  62.4 7.4 %copy-start.30 = (f32[1536]{0:T(1024)S(1)}, f32[1536]{0:T(1024)}, u32[]{:S(2)}) copy-start(f32[1536]{0:T(1024)} %param.20) | copy-start | bytes 18436
  62.5 48.3 %all-to-all-start.1 = ((bf16[8,4,57344]{2,1,0:T(4,128)(2,1)}), bf16[8,4,57344]{2,1,0:T(4,128)(2,1)}, u32[]{:S(2)}, u32[]{:S(2)}) async-start(bf16[8,4,57344]{2,1,0:T(4,128)(2,1)} %broadcast_in_dim.172), calls=%async_computation.1 | async-start | bytes 7340032 | tf_op jit(solution)/shard_map/all_to_all | solution.py:122
  69.6 48.3 %copy-start.25 = (f32[256]{0:T(256)}, f32[256]{0:T(256)S(1)}, u32[]{:S(2)}) copy-start(f32[256]{0:T(256)S(1)} %add_rsqrt_fusion) | copy-start | bytes 3076
  127.5 5.8 %copy-start.15 = (s32[2048]{0:T(1024)S(1)}, s32[2048]{0:T(1024)}, u32[]{:S(2)}) copy-start(s32[2048]{0:T(1024)} %convert_reduce_fusion) | copy-start | bytes 24580
  127.5 5.8 %copy-start.17 = (s32[256]{0:T(256)S(1)}, s32[256]{0:T(256)}, u32[]{:S(2)}) copy-start(s32[256]{0:T(256)} %copy-done.16) | copy-start | bytes 3076
  127.5 5.8 %copy-start.21 = (s32[256]{0:T(256)S(1)}, s32[256]{0:T(256)}, u32[]{:S(2)}) copy-start(s32[256]{0:T(256)} %copy-done.20) | copy-start | bytes 3076
  128.6 19.6 %all-to-all-start.2 = ((bf16[8,256,256]{1,2,0:T(8,128)(2,1)}), bf16[8,256,256]{1,2,0:T(8,128)(2,1)S(1)}, u32[]{:S(2)}, u32[]{:S(2)}) async-start(bf16[8,256,256]{1,2,0:T(8,128)(2,1)} %broadcast_in_dim.174), calls=%async_computation.2 | async-start | bytes 2097152 | tf_op jit(solution)/shard_map/all_to_all | solution.py:169
  161.8 5.9 %copy-start.19 = (s32[4,128]{1,0:T(4,128)S(1)}, s32[4,128]{1,0:T(4,128)}, u32[]{:S(2)}) copy-start(s32[4,128]{1,0:T(4,128)} %eq.130) | copy-start | bytes 6148
  161.8 5.9 %copy-start.8 = (s32[64,8]{1,0:T(8,128)S(1)}, s32[64,8]{1,0:T(8,128)}, u32[]{:S(2)}) copy-start(s32[64,8]{1,0:T(8,128)} %copy-done.7) | copy-start | bytes 6148
  163.3 15.7 %copy-start.18 = (f32[1536]{0:T(1024)S(1)}, f32[1536]{0:T(1024)}, u32[]{:S(2)}) copy-start(f32[1536]{0:T(1024)} %param.32) | copy-start | bytes 18436
  163.3 14.4 %all-to-all-start.3 = ((bf16[4,64,1536]{2,1,0:T(8,128)(2,1)}), bf16[4,64,1536]{2,1,0:T(8,128)(2,1)S(1)}, u32[]{:S(2)}, u32[]{:S(2)}) async-start(bf16[4,64,1536]{2,1,0:T(8,128)(2,1)} %bitcast.31), calls=%async_computation.3 | async-start | bytes 1572864 | tf_op jit(solution)/shard_map/all_to_all | solution.py:204
  186.4 55.7 %all-to-all-start.4 = ((bf16[8,160,1536]{2,0,1:T(8,128)(2,1)}), bf16[8,160,1536]{2,0,1:T(8,128)(2,1)}, u32[]{:S(2)}, u32[]{:S(2)}) async-start(bf16[8,160,1536]{2,0,1:T(8,128)(2,1)} %bitcast.211), calls=%async_computation.4 | async-start | bytes 7864320 | tf_op jit(solution)/shard_map/all_to_all | solution.py:239
  245.6 53.2 %all-to-all-start.6 = ((bf16[8,160,1536]{2,0,1:T(8,128)(2,1)}), bf16[8,160,1536]{2,0,1:T(8,128)(2,1)}, u32[]{:S(2)}, u32[]{:S(2)}) async-start(bf16[8,160,1536]{2,0,1:T(8,128)(2,1)} %bitcast.210), calls=%async_computation.6 | async-start | bytes 7864320 | tf_op jit(solution)/shard_map/all_to_all | solution.py:239
  298.8 53.1 %all-to-all-start.5 = ((bf16[8,160,1536]{2,0,1:T(8,128)(2,1)}), bf16[8,160,1536]{2,0,1:T(8,128)(2,1)}, u32[]{:S(2)}, u32[]{:S(2)}) async-start(bf16[8,160,1536]{2,0,1:T(8,128)(2,1)} %bitcast.209), calls=%async_computation.5 | async-start | bytes 7864320 | tf_op jit(solution)/shard_map/all_to_all | solution.py:246
  351.9 5.7 %copy-start.23 = (f32[64,8]{0,1:T(8,128)S(1)}, f32[64,8]{0,1:T(8,128)}, u32[]{:S(2)}) copy-start(f32[64,8]{0,1:T(8,128)} %param.34) | copy-start | bytes 6148
  351.9 5.8 %copy-start.11 = (s32[64,8]{1,0:T(8,128)S(1)}, s32[64,8]{1,0:T(8,128)}, u32[]{:S(2)}) copy-start(s32[64,8]{1,0:T(8,128)} %copy-done.10) | copy-start | bytes 6148
  351.9 53.4 %all-to-all-start.7 = ((bf16[8,160,1536]{2,0,1:T(8,128)(2,1)}), bf16[8,160,1536]{2,0,1:T(8,128)(2,1)}, u32[]{:S(2)}, u32[]{:S(2)}) async-start(bf16[8,160,1536]{2,0,1:T(8,128)(2,1)} %bitcast.208), calls=%async_computation.7 | async-start | bytes 7864320 | tf_op jit(solution)/shard_map/all_to_all | solution.py:246
  (19 other events, 56.8 us)
